TPU v7x, 256 devices: a whole 4x4x8 slice. The times are simulated.
256 devices in a mesh: leaf: 4 (over y), row: 8 (over z), col: 8 (over x, core).
Axes of the slice: x: 4, y: 4, z: 8, core: 2. Of those that a mesh axis runs over, the one named last changes fastest.
Arguments:
- rhs: float32 [4, 4, 8, 256, 256], P('leaf', None, 'row'), may hold values from -6 to 6
- rhs_top: float32 [2, 8, 256, 256], P(None, 'row'), may hold values from -6 to 6
- factor: bfloat16 [4, 4, 8, 4, 8, 256, 256], P('leaf', None, 'row', None, 'col'), may hold values from -0.125 to 0.125
- factor_inv: bfloat16 [4, 2, 4, 8, 256, 256], P('leaf', None, None, 'row')
- lower_bridge: bfloat16 [4, 2, 8, 4, 8, 256, 256], P('leaf', None, 'row', None, 'col'), may hold values from -0.0625 to 0.0625
- upper_bridge: bfloat16 [4, 4, 8, 2, 8, 256, 256], P('leaf', None, 'row', None, 'col'), may hold values from -0.1875 to 0.1875
- top_factor: bfloat16 [2, 8, 2, 8, 256, 256], P(None, 'row', None, 'col'), may hold values from -0.1875 to 0.1875
- top_inv: bfloat16 [2, 2, 8, 256, 256], P(None, None, 'row')
- widths: int32 [4, 4, 8], P('leaf', None, 'row'), may hold values from 128 to 256, as said below
- pattern: int32 [4, 4, 8, 4, 8], P('leaf', None, 'row', None, 'col'), may hold values 0 or 1
- lower_links: int32 [4, 2, 8, 4, 8], P('leaf', None, 'row', None, 'col'), may hold values 0 or 1
- upper_links: int32 [4, 4, 8, 2, 8], P('leaf', None, 'row', None, 'col'), may hold values 0 or 1
- top_pattern: int32 [2, 8, 2, 8], P(None, 'row', None, 'col'), may hold values 0 or 1
Outputs:
- solution: float32 [4, 4, 8, 256, 256], P('leaf', None, 'row', None, 'col')
- solution_top: float32 [2, 8, 256, 256], P(None, 'row', None, 'col')
Inputs may be any that keep to these rules, and one draw needn't show every extreme that they name: widths of supernodes; the largest is 256 in every subtree.
All inputs are finite; a program needn't handle non-finite values. No bound on the sum of `pattern` or of `lower_links` or of `upper_links` or of `top_pattern` on one device may be relied on, other than what follows from the above.
Results may differ from a plain program's by a relative error of at most 0.02.
Values may be sent and summed in bfloat16 or wider, within the bound.
No kernel may reach another device: no remote copies, remote signals or barrier semaphores. Data moves between devices by JAX's collectives and lax.ppermute only.
A program may use at most 64 MiB of HBM per device.

v0:
```python
import jax
import jax.numpy as jnp
from jax import lax
from jax.sharding import PartitionSpec as P


def masked(blocks, marks):
    return blocks * marks.astype(jnp.bfloat16)[..., None, None]


def column_part(full, width):
    start = lax.axis_index("col") * width
    return lax.dynamic_slice_in_dim(full, start, width, 0)


def settle(partial_value, target, inverse, keep):
    share = lax.psum_scatter(partial_value, "col", scatter_dimension=2, tiled=True)
    resid = (target - share).astype(jnp.bfloat16)
    solved = keep * jnp.einsum("ibk,ikr->ibr", inverse, resid, preferred_element_type=jnp.float32)
    pieces = lax.all_gather(solved.astype(jnp.bfloat16)[None], ("row", "col"), axis=0, tiled=True)
    nrows = lax.axis_size("row")
    ncols = lax.axis_size("col")
    pieces = pieces.reshape((nrows, ncols) + solved.shape)
    full = jnp.transpose(pieces, (0, 2, 3, 1, 4)).reshape(
        nrows * solved.shape[0], solved.shape[1], ncols * solved.shape[2]
    )
    return (solved, full)


def shards(
    rhs,
    rhs_top,
    factor,
    factor_inv,
    lower_bridge,
    upper_bridge,
    top_factor,
    top_inv,
    widths,
    pattern,
    lower_links,
    upper_links,
    top_pattern,
):
    f32 = jnp.float32
    levels = factor.shape[1]
    tops = top_factor.shape[0]
    row_count = factor.shape[2]
    col_count = factor.shape[4]
    block = factor.shape[5]
    sides = rhs.shape[4]
    share_width = sides // lax.axis_size("col")
    col_start = lax.axis_index("col") * share_width
    local_rhs = lax.dynamic_slice_in_dim(rhs[0], col_start, share_width, 3)
    local_top = lax.dynamic_slice_in_dim(rhs_top, col_start, share_width, 3)
    fmask = masked(factor[0], pattern[0])
    lmask = masked(lower_bridge[0], lower_links[0])
    umask = masked(upper_bridge[0], upper_links[0])
    tmask = masked(top_factor, top_pattern)
    marks = lax.broadcasted_iota(jnp.int32, (levels, row_count, block, 1), 2)
    keep = (marks < widths[0][..., None, None]).astype(f32)
    ys = []
    ycols = []
    for level in range(levels):
        if level == 0:
            partial_value = jnp.zeros((row_count, block, sides), f32)
        else:
            partial_value = jnp.einsum(
                "iljbk,ljkr->ibr",
                fmask[level, :, :level],
                jnp.stack(ycols, 0),
                preferred_element_type=f32,
            )
        solved, full = settle(partial_value, local_rhs[level], factor_inv[0, 0, level], keep[level])
        ys.append(solved)
        ycols.append(column_part(full, col_count))
    coupling = jnp.einsum(
        "tiljbk,ljkr->tibr", lmask, jnp.stack(ycols, 0), preferred_element_type=f32
    )
    coupling = lax.psum(coupling, "leaf")
    yts = []
    tcols = []
    for top in range(tops):
        partial_value = coupling[top]
        if top > 0:
            partial_value = partial_value + jnp.einsum(
                "iljbk,ljkr->ibr",
                tmask[top, :, :top],
                jnp.stack(tcols, 0),
                preferred_element_type=f32,
            )
        solved, full = settle(partial_value, local_top[top], top_inv[0, top], 1.0)
        yts.append(solved)
        tcols.append(column_part(full, col_count))
    zts = [None] * tops
    zt_cols = [None] * tops
    for top in reversed(range(tops)):
        if top == tops - 1:
            partial_value = jnp.zeros((row_count, block, sides), f32)
        else:
            partial_value = jnp.einsum(
                "iljbk,ljkr->ibr",
                tmask[top, :, top + 1 :],
                jnp.stack(zt_cols[top + 1 :], 0),
                preferred_element_type=f32,
            )
        solved, full = settle(partial_value, yts[top], top_inv[1, top], 1.0)
        zts[top] = solved
        zt_cols[top] = column_part(full, col_count)
    top_stack = jnp.stack(zt_cols, 0)
    zs = [None] * levels
    zcols = [None] * levels
    for level in reversed(range(levels)):
        partial_value = jnp.einsum(
            "itjbk,tjkr->ibr", umask[level], top_stack, preferred_element_type=f32
        )
        if level < levels - 1:
            partial_value = partial_value + jnp.einsum(
                "iljbk,ljkr->ibr",
                fmask[level, :, level + 1 :],
                jnp.stack(zcols[level + 1 :], 0),
                preferred_element_type=f32,
            )
        solved, full = settle(partial_value, ys[level], factor_inv[0, 1, level], keep[level])
        zs[level] = solved
        zcols[level] = column_part(full, col_count)
    result = jnp.stack(zs, 0)
    result_top = jnp.stack(zts, 0)
    return (result[None], result_top)


def solution(mesh):
    placed = (
        P("leaf", None, "row", None, None),
        P(None, "row", None, None),
        P("leaf", None, "row", None, "col", None, None),
        P("leaf", None, None, "row", None, None),
        P("leaf", None, "row", None, "col", None, None),
        P("leaf", None, "row", None, "col", None, None),
        P(None, "row", None, "col", None, None),
        P(None, None, "row", None, None),
        P("leaf", None, "row"),
        P("leaf", None, "row", None, "col"),
        P("leaf", None, "row", None, "col"),
        P("leaf", None, "row", None, "col"),
        P(None, "row", None, "col"),
    )
    return jax.shard_map(
        shards,
        mesh=mesh,
        in_specs=placed,
        out_specs=(P("leaf", None, "row", None, "col"), P(None, "row", None, "col")),
        check_vma=False,
    )
```

profile of v0, /device:TPU:8, one launch (start us, length us, event | category | flops | bytes accessed | tf_op | source)
XLA Modules:
  0.0 1329.3 jit_solution(12221357856252894785)
XLA Ops:
  7.2 1.2 copy-done
  9.5 1.7 bitcast_convert_fusion.9
  12.0 1.8 bitcast_multiply_fusion
  13.8 70.6 %all-gather.21.cloned.1.call-done = bf16[16384,32]{0,1:T(8,128)(2,1)} async-done(((bf16[256,32]{0,1:T(8,128)(2,1)}), bf16[16384,32]{0,1:T(8,128)(2,1)}) %all-gather.21.cloned.1.call-update) | async-done | bytes 1048592 | tf_op jit(solution)/shard_map/all_gather | solution.py:20
  84.4 1.5 copy.160
  87.6 1.7 fusion.99
  89.4 1.6 copy.157
  90.9 1.3 dynamic-slice.1
  92.9 59.3 %all-reduce.14.cloned.1.call-done = f32[1,256,256]{1,0,2:T(1,128)} async-done(((f32[1,256,256]{1,0,2:T(1,128)}), f32[1,256,256]{1,0,2:T(1,128)}) %all-reduce.14.cloned.1.call-update) | async-done | bytes 262160
  153.0 1.7 bitcast_convert_fusion.8
  155.5 69.2 %all-gather.23.cloned.1.call-done = bf16[16384,32]{0,1:T(8,128)(2,1)} async-done(((bf16[256,32]{0,1:T(8,128)(2,1)}), bf16[16384,32]{0,1:T(8,128)(2,1)}) %all-gather.23.cloned.1.call-update) | async-done | bytes 1048592 | tf_op jit(solution)/shard_map/all_gather | solution.py:20
  224.7 1.5 copy.161
  227.6 1.9 convolution_bitcast_fusion.8
  229.5 1.8 copy.101
  231.4 64.5 %all-reduce.16.cloned.1.call-done = f32[1,256,256]{1,0,2:T(1,128)} async-done(((f32[1,256,256]{1,0,2:T(1,128)}), f32[1,256,256]{1,0,2:T(1,128)}) %all-reduce.16.cloned.1.call-update) | async-done | bytes 262160
  296.6 1.7 bitcast_convert_fusion.7
  298.4 69.4 %all-gather.25.cloned.1.call-done = bf16[16384,32]{0,1:T(8,128)(2,1)} async-done(((bf16[256,32]{0,1:T(8,128)(2,1)}), bf16[16384,32]{0,1:T(8,128)(2,1)}) %all-gather.25.cloned.1.call-update) | async-done | bytes 1048592 | tf_op jit(solution)/shard_map/all_gather | solution.py:20
  367.8 1.5 copy.162
  370.7 2.0 convolution_bitcast_fusion.7
  372.6 1.8 copy.105
  374.6 64.5 %all-reduce.18.cloned.1.call-done = f32[1,256,256]{1,0,2:T(1,128)} async-done(((f32[1,256,256]{1,0,2:T(1,128)}), f32[1,256,256]{1,0,2:T(1,128)}) %all-reduce.18.cloned.1.call-update) | async-done | bytes 262160
  439.8 1.7 bitcast_convert_fusion.6
  442.8 68.2 %all-gather.27.cloned.1.call-done = bf16[16384,32]{0,1:T(8,128)(2,1)} async-done(((bf16[256,32]{0,1:T(8,128)(2,1)}), bf16[16384,32]{0,1:T(8,128)(2,1)}) %all-gather.27.cloned.1.call-update) | async-done | bytes 1048592 | tf_op jit(solution)/shard_map/all_gather | solution.py:20
  511.0 1.5 copy.163
  513.9 2.6 convolution_bitcast_fusion
  516.5 46.4 %all-reduce.12.cloned.1.call-done = f32[2,1,256,256]{3,2,0,1:T(8,128)} async-done(((f32[2,1,256,256]{3,2,0,1:T(8,128)}), f32[2,1,256,256]{3,2,0,1:T(8,128)}) %all-reduce.12.cloned.1.call-update) | async-done | bytes 524304 | tf_op jit(solution)/shard_map/psum | solution.py:80
  564.8 1.1 constant_dynamic-slice_fusion.10
  566.0 66.3 %all-reduce.20.cloned.1.call-done = f32[1,256,256]{1,0,2:T(1,128)} async-done(((f32[1,256,256]{1,0,2:T(1,128)}), f32[1,256,256]{1,0,2:T(1,128)}) %all-reduce.20.cloned.1.call-update) | async-done | bytes 262160
  633.0 1.7 bitcast_convert_fusion.5
  635.5 1.9 broadcast_multiply_fusion
  637.5 66.7 %all-gather.29.cloned.1.call-done = bf16[16384,32]{0,1:T(8,128)(2,1)} async-done(((bf16[256,32]{0,1:T(8,128)(2,1)}), bf16[16384,32]{0,1:T(8,128)(2,1)}) %all-gather.29.cloned.1.call-update) | async-done | bytes 1048592 | tf_op jit(solution)/shard_map/all_gather | solution.py:20
  704.2 1.5 copy.164
  706.3 1.1 fusion.1
  708.4 64.5 %all-reduce.22.cloned.1.call-done = f32[1,256,256]{1,0,2:T(1,128)} async-done(((f32[1,256,256]{1,0,2:T(1,128)}), f32[1,256,256]{1,0,2:T(1,128)}) %all-reduce.22.cloned.1.call-update) | async-done | bytes 262160
  773.7 1.9 bitcast_convert_fusion.4
  775.7 69.4 %all-gather.31.cloned.1.call-done = bf16[16384,32]{0,1:T(8,128)(2,1)} async-done(((bf16[256,32]{0,1:T(8,128)(2,1)}), bf16[16384,32]{0,1:T(8,128)(2,1)}) %all-gather.31.cloned.1.call-update) | async-done | bytes 1048592 | tf_op jit(solution)/shard_map/all_gather | solution.py:20
  845.1 1.5 copy.165
  847.2 1.8 convolution_bitcast_fusion.9
  849.1 32.6 %reduce-scatter.6.cloned.1.call-done = f32[1,256,32]{1,2,0:T(8,128)} async-done(((f32[1,256,256]{1,2,0:T(8,128)}), f32[1,256,32]{1,2,0:T(8,128)}) %reduce-scatter.6.cloned.1.call-update) | async-done | bytes 32784 | tf_op jit(solution)/shard_map/reduce_scatter | solution.py:17
  881.7 1.7 bitcast_convert_fusion.3
  883.6 2.4 bitcast_multiply_fusion.3
  886.1 67.7 %all-gather.33.cloned.1.call-done = bf16[16384,32]{0,1:T(8,128)(2,1)} async-done(((bf16[256,32]{0,1:T(8,128)(2,1)}), bf16[16384,32]{0,1:T(8,128)(2,1)}) %all-gather.33.cloned.1.call-update) | async-done | bytes 1048592 | tf_op jit(solution)/shard_map/all_gather | solution.py:20
  953.8 1.5 copy.166
  956.0 1.9 convolution_bitcast_fusion.3
  958.0 32.6 %reduce-scatter.8.cloned.1.call-done = f32[1,256,32]{1,2,0:T(8,128)} async-done(((f32[1,256,256]{1,2,0:T(8,128)}), f32[1,256,32]{1,2,0:T(8,128)}) %reduce-scatter.8.cloned.1.call-update) | async-done | bytes 32784 | tf_op jit(solution)/shard_map/reduce_scatter | solution.py:17
  990.7 1.7 bitcast_convert_fusion.2
  992.7 2.0 convolution_bitcast_fusion.4
  994.6 68.2 %all-gather.35.cloned.1.call-done = bf16[16384,32]{0,1:T(8,128)(2,1)} async-done(((bf16[256,32]{0,1:T(8,128)(2,1)}), bf16[16384,32]{0,1:T(8,128)(2,1)}) %all-gather.35.cloned.1.call-update) | async-done | bytes 1048592 | tf_op jit(solution)/shard_map/all_gather | solution.py:20
  1062.8 1.5 copy.167
  1066.0 32.6 %reduce-scatter.10.cloned.1.call-done = f32[1,256,32]{1,2,0:T(8,128)} async-done(((f32[1,256,256]{1,2,0:T(8,128)}), f32[1,256,32]{1,2,0:T(8,128)}) %reduce-scatter.10.cloned.1.call-update) | async-done | bytes 32784 | tf_op jit(solution)/shard_map/reduce_scatter | solution.py:17
  1098.6 1.7 bitcast_convert_fusion.1
  1101.1 69.0 %all-gather.37.cloned.1.call-done = bf16[16384,32]{0,1:T(8,128)(2,1)} async-done(((bf16[256,32]{0,1:T(8,128)(2,1)}), bf16[16384,32]{0,1:T(8,128)(2,1)}) %all-gather.37.cloned.1.call-update) | async-done | bytes 1048592 | tf_op jit(solution)/shard_map/all_gather | solution.py:20
  1170.1 1.5 copy.168
  1173.0 1.2 convolution_bitcast_fusion.2
  1174.2 2.0 fusion.5
  1176.3 32.6 %reduce-scatter.12.cloned.1.call-done = f32[1,256,32]{1,2,0:T(8,128)} async-done(((f32[1,256,256]{1,2,0:T(8,128)}), f32[1,256,32]{1,2,0:T(8,128)}) %reduce-scatter.12.cloned.1.call-update) | async-done | bytes 32784 | tf_op jit(solution)/shard_map/reduce_scatter | solution.py:17
  1208.9 1.7 bitcast_convert_fusion
  1210.7 70.3 %all-gather.39.cloned.1.call-done = bf16[16384,32]{0,1:T(8,128)(2,1)} async-done(((bf16[256,32]{0,1:T(8,128)(2,1)}), bf16[16384,32]{0,1:T(8,128)(2,1)}) %all-gather.39.cloned.1.call-update) | async-done | bytes 1048592 | tf_op jit(solution)/shard_map/all_gather | solution.py:20
  1281.0 1.5 copy.169
  1283.9 1.4 convolution_bitcast_fusion.1
  1285.3 1.9 fusion.3
  1287.9 32.0 %reduce-scatter.14.cloned.1.call-done = f32[1,256,32]{1,2,0:T(8,128)} async-done(((f32[1,256,256]{1,2,0:T(8,128)}), f32[1,256,32]{1,2,0:T(8,128)}) %reduce-scatter.14.cloned.1.call-update) | async-done | bytes 32784 | tf_op jit(solution)/shard_map/reduce_scatter | solution.py:17
  1319.9 1.1 fusion.6
  1321.0 1.5 maximum_bitcast_fusion.11
  (124 shorter events, 26.1 us)
Async XLA Ops:
  7.2 1.2 copy-start
  7.2 77.2 %all-gather.21.cloned.1.call-start = ((), (), s32[]{:S(2)}) async-start(), calls=%async_computation.11 | async-start | bytes 1064960 | tf_op jit(solution)/shard_map/all_gather | solution.py:20
  8.6 3.4 copy-start.1
  11.2 141.0 %all-reduce.14.cloned.1.call-start = ((), (), s32[]{:S(2)}) async-start(), calls=%async_computation.21 | async-start | bytes 524288
  87.6 137.1 %all-gather.23.cloned.1.call-start = ((), (), s32[]{:S(2)}) async-start(), calls=%async_computation.12 | async-start | bytes 1064960 | tf_op jit(solution)/shard_map/all_gather | solution.py:20
  154.7 141.2 %all-reduce.16.cloned.1.call-start = ((), (), s32[]{:S(2)}) async-start(), calls=%async_computation.22 | async-start | bytes 524288
  231.3 136.5 %all-gather.25.cloned.1.call-start = ((), (), s32[]{:S(2)}) async-start(), calls=%async_computation.13 | async-start | bytes 1064960 | tf_op jit(solution)/shard_map/all_gather | solution.py:20
  298.4 140.7 %all-reduce.18.cloned.1.call-start = ((), (), s32[]{:S(2)}) async-start(), calls=%async_computation.23 | async-start | bytes 524288
  367.8 2.9 copy-start.6
  374.5 136.5 %all-gather.27.cloned.1.call-start = ((), (), s32[]{:S(2)}) async-start(), calls=%async_computation.14 | async-start | bytes 1064960 | tf_op jit(solution)/shard_map/all_gather | solution.py:20
  441.5 121.4 %all-reduce.12.cloned.1.call-start = ((), (), s32[]{:S(2)}) async-start(), calls=%async_computation.5 | async-start | bytes 1048576 | tf_op jit(solution)/shard_map/psum | solution.py:80
  511.0 2.9 copy-start.7
  516.5 115.8 %all-reduce.20.cloned.1.call-start = ((), (), s32[]{:S(2)}) async-start(), calls=%async_computation.24 | async-start | bytes 524288
  564.7 139.4 %all-gather.29.cloned.1.call-start = ((), (), s32[]{:S(2)}) async-start(), calls=%async_computation.15 | async-start | bytes 1064960 | tf_op jit(solution)/shard_map/all_gather | solution.py:20
  634.8 138.2 %all-reduce.22.cloned.1.call-start = ((), (), s32[]{:S(2)}) async-start(), calls=%async_computation.25 | async-start | bytes 524288
  704.2 2.1 copy-start.2
  708.3 136.7 %all-gather.31.cloned.1.call-start = ((), (), s32[]{:S(2)}) async-start(), calls=%async_computation.16 | async-start | bytes 1064960 | tf_op jit(solution)/shard_map/all_gather | solution.py:20
  775.6 106.1 %reduce-scatter.6.cloned.1.call-start = ((), (), s32[]{:S(2)}) async-start(), calls=%async_computation.6 | async-start | bytes 294912 | tf_op jit(solution)/shard_map/reduce_scatter | solution.py:17
  846.5 35.2 %copy-start.5 = (f32[32,256]{1,0:T(8,128)S(1)}, f32[32,256]{1,0:T(8,128)}, u32[]{:S(2)}) copy-start(f32[32,256]{1,0:T(8,128)} %get-tuple-element.28) | copy-start | bytes 98308
  846.5 37.0 %copy-start.12 = (s32[1,4,1,2,1]{1,4,3,2,0:T(1,128)S(1)}, s32[1,4,1,2,1]{1,4,3,2,0:T(1,128)}, u32[]{:S(2)}) copy-start(s32[1,4,1,2,1]{1,4,3,2,0:T(1,128)} %param.24) | copy-start | bytes 100
  849.0 104.8 %all-gather.33.cloned.1.call-start = ((), (), s32[]{:S(2)}) async-start(), calls=%async_computation.17 | async-start | bytes 1064960 | tf_op jit(solution)/shard_map/all_gather | solution.py:20
  883.4 107.2 %reduce-scatter.8.cloned.1.call-start = ((), (), s32[]{:S(2)}) async-start(), calls=%async_computation.7 | async-start | bytes 294912 | tf_op jit(solution)/shard_map/reduce_scatter | solution.py:17
  958.0 104.8 %all-gather.35.cloned.1.call-start = ((), (), s32[]{:S(2)}) async-start(), calls=%async_computation.18 | async-start | bytes 1064960 | tf_op jit(solution)/shard_map/all_gather | solution.py:20
  992.4 106.1 %reduce-scatter.10.cloned.1.call-start = ((), (), s32[]{:S(2)}) async-start(), calls=%async_computation.8 | async-start | bytes 294912 | tf_op jit(solution)/shard_map/reduce_scatter | solution.py:17
  1062.8 2.1 copy-start.3
  1065.9 104.2 %all-gather.37.cloned.1.call-start = ((), (), s32[]{:S(2)}) async-start(), calls=%async_computation.19 | async-start | bytes 1064960 | tf_op jit(solution)/shard_map/all_gather | solution.py:20
  1100.3 108.6 %reduce-scatter.12.cloned.1.call-start = ((), (), s32[]{:S(2)}) async-start(), calls=%async_computation.9 | async-start | bytes 294912 | tf_op jit(solution)/shard_map/reduce_scatter | solution.py:17
  1173.0 35.9 %copy-start.4 = (f32[32,256]{1,0:T(8,128)S(1)}, f32[32,256]{1,0:T(8,128)}, u32[]{:S(2)}) copy-start(f32[32,256]{1,0:T(8,128)} %get-tuple-element.22) | copy-start | bytes 98308
  1176.2 104.8 %all-gather.39.cloned.1.call-start = ((), (), s32[]{:S(2)}) async-start(), calls=%async_computation.20 | async-start | bytes 1064960 | tf_op jit(solution)/shard_map/all_gather | solution.py:20
  1210.6 109.3 %reduce-scatter.14.cloned.1.call-start = ((), (), s32[]{:S(2)}) async-start(), calls=%async_computation.10 | async-start | bytes 294912 | tf_op jit(solution)/shard_map/reduce_scatter | solution.py:17
  1283.9 3.4 copy-start.9
  1283.9 3.4 copy-start.10
  1283.9 36.0 %copy-start.8 = (f32[32,256]{1,0:T(8,128)S(1)}, f32[32,256]{1,0:T(8,128)}, u32[]{:S(2)}) copy-start(f32[32,256]{1,0:T(8,128)} %get-tuple-element.20) | copy-start | bytes 98308
  1283.9 37.1 %copy-start.11 = (f32[32,256]{1,0:T(8,128)S(1)}, f32[32,256]{1,0:T(8,128)}, u32[]{:S(2)}) copy-start(f32[32,256]{1,0:T(8,128)} %get-tuple-element.34) | copy-start | bytes 98308
Sparse Core Ops, SparseCore 0:
  11.3 73.0 all-gather.20
  87.7 64.4 all-reduce.13
  155.4 69.2 all-gather.22
  231.4 64.4 all-reduce.15
  298.5 69.2 all-gather.24
  374.6 64.4 all-reduce.17
  441.7 69.2 all-gather.26
  516.6 46.2 all-reduce.11
  565.2 66.9 all-reduce.19
  634.9 69.2 all-gather.28
  708.5 64.4 all-reduce.21
  775.7 69.2 all-gather.30
  849.1 32.4 reduce-scatter.5
  884.8 69.0 all-gather.32
  958.1 32.4 reduce-scatter.7
  993.7 69.0 all-gather.34
  1066.0 32.4 reduce-scatter.9
  1101.1 69.0 all-gather.36
  1176.3 32.4 reduce-scatter.11
  1212.0 69.0 all-gather.38
  1287.3 32.4 reduce-scatter.13
where the time goes:
time: 1330 us
  waiting for transfers between devices  1220 us (92%)
  local copies, waits for them, and re-layouts  45.3 us (3%)
  matrix products  39.4 us (3%)
  between operations  15.4 us (1%)
    all_gather x10, waiting for transfers between devices, settle(): lax.all_gather(solved.astype(jnp.bfloat16)[None], ('row', 'col'), axis=0,...  689 us
    unnamed x26, waiting for transfers between devices  319 us
    reduce_scatter x5, waiting for transfers between devices, settle(): lax.psum_scatter(partial_value, 'col', scatter_dimension=2, tiled=True)  162 us
    psum x1, waiting for transfers between devices, shards(): coupling = lax.psum(coupling, 'leaf')  46.4 us
  transfers between devices with their start and end apart: 21, of which 21 were waited for; matrix products, arithmetic and copies ran while one was open for 1% of the time, Pallas kernels for 0%

commit v1 on v0

--- a/solution.py
+++ b/solution.py
@@ -17,7 +17,15 @@
     share = lax.psum_scatter(partial_value, "col", scatter_dimension=2, tiled=True)
     resid = (target - share).astype(jnp.bfloat16)
     solved = keep * jnp.einsum("ibk,ikr->ibr", inverse, resid, preferred_element_type=jnp.float32)
-    pieces = lax.all_gather(solved.astype(jnp.bfloat16)[None], ("row", "col"), axis=0, tiled=True)
+    pieces = jnp.concatenate(
+        lax.all_to_all(
+            jnp.stack([solved.astype(jnp.bfloat16)[None]] * lax.axis_size(("row", "col"))),
+            ("row", "col"),
+            0,
+            0,
+        ),
+        axis=0,
+    )
     nrows = lax.axis_size("row")
     ncols = lax.axis_size("col")
     pieces = pieces.reshape((nrows, ncols) + solved.shape)

time: 1330 us -> 970 us (0.73)
  waiting for transfers between devices: 1220 us -> 691 us
  blocking collectives: 0 us -> 110 us
  starting transfers between devices: 1.06 us -> 63.4 us
    all_gather x10 -> x0, waiting for transfers between devices: 689 us -> none  [settle(): lax.all_gather(solved.astype(jnp.bfloat16)[None], ('row', 'col'), axis=0,...]
    all_to_all x0 -> x7, waiting for transfers between devices: none -> 190 us  [settle(): lax.all_to_all(jnp.stack([solved.astype(jnp.bfloat16)[None]] * lax.axis_s...]
    all_to_all x0 -> x3, blocking collectives: none -> 110 us  [settle(): lax.all_to_all(jnp.stack([solved.astype(jnp.bfloat16)[None]] * lax.axis_s...]
    all_to_all x0 -> x7, starting transfers between devices: none -> 62.9 us  [settle(): lax.all_to_all(jnp.stack([solved.astype(jnp.bfloat16)[None]] * lax.axis_s...]
    unnamed x51 -> x43, local copies, waits for them, and re-layouts: 23.5 us -> 8.79 us
    reduce_scatter x5, waiting for transfers between devices: 162 us -> 149 us  [settle(): lax.psum_scatter(partial_value, 'col', scatter_dimension=2, tiled=True)]
    unnamed x26 -> x16, waiting for transfers between devices: 319 us -> 309 us
  transfers between devices with their start and end apart: 21 -> 18, of which waited for: 21 -> 18; matrix products, arithmetic and copies ran while one was open for 1% -> 2% of each run, Pallas kernels for 0% -> 0%
where the time goes in v1:
time: 970 us; the launch traced here: 967 us
  waiting for transfers between devices  691 us (71%)
  blocking collectives  110 us (11%)
  starting transfers between devices  63.4 us (7%)
  matrix products  40.3 us (4%)
  local copies, waits for them, and re-layouts  38 us (4%)
  between operations  14.9 us (2%)
    unnamed x16, waiting for transfers between devices  309 us
    all_to_all x7, waiting for transfers between devices, settle(): lax.all_to_all(jnp.stack([solved.astype(jnp.bfloat16)[None]] * lax.axis_s...  190 us
    reduce_scatter x5, waiting for transfers between devices, settle(): lax.psum_scatter(partial_value, 'col', scatter_dimension=2, tiled=True)  149 us
    all_to_all x3, blocking collectives, settle(): lax.all_to_all(jnp.stack([solved.astype(jnp.bfloat16)[None]] * lax.axis_s...  110 us
    all_to_all x7, starting transfers between devices, settle(): lax.all_to_all(jnp.stack([solved.astype(jnp.bfloat16)[None]] * lax.axis_s...  62.9 us
    psum x1, waiting for transfers between devices, shards(): coupling = lax.psum(coupling, 'leaf')  43.7 us
  transfers between devices with their start and end apart: 18, of which 18 were waited for; matrix products, arithmetic and copies ran while one was open for 2% of the time, Pallas kernels for 0%

profile of v1, /device:TPU:8, one launch (start us, length us, event | category | flops | bytes accessed | tf_op | source)
XLA Modules:
  0.0 967.4 jit_solution(13038042623170762899)
XLA Ops:
  7.2 1.2 copy-done
  9.5 1.7 bitcast_convert_fusion.9
  12.3 12.2 %all-to-all-start = ((bf16[64,1,1,256,32]{3,4,2,1,0:T(8,128)(2,1)}), bf16[64,1,1,256,32]{3,4,2,1,0:T(8,128)(2,1)}, u32[]{:S(2)}, u32[]{:S(2)}) async-start(bf16[64,1,1,256,32]{3,4,2,1,0:T(8,128)(2,1)} %stack.110), calls=%async_computation | async-start | bytes 2097152 | tf_op jit(solution)/shard_map/all_to_all | solution.py:21
  24.6 1.8 bitcast_multiply_fusion
  26.4 26.8 %all-to-all-done = bf16[64,1,1,256,32]{3,4,2,1,0:T(8,128)(2,1)} async-done(((bf16[64,1,1,256,32]{3,4,2,1,0:T(8,128)(2,1)}), bf16[64,1,1,256,32]{3,4,2,1,0:T(8,128)(2,1)}, u32[]{:S(2)}, u32[]{:S(2)}) %all-to-all-start) | async-done | bytes 1048608 | tf_op jit(solution)/shard_map/all_to_all | solution.py:21
  55.2 1.7 fusion.99
  56.9 1.6 copy.137
  58.5 1.3 dynamic-slice.1
  60.4 56.8 %all-reduce.14.cloned.1.call-done = f32[1,256,256]{1,0,2:T(1,128)} async-done(((f32[1,256,256]{1,0,2:T(1,128)}), f32[1,256,256]{1,0,2:T(1,128)}) %all-reduce.14.cloned.1.call-update) | async-done | bytes 262160
  118.0 1.7 bitcast_convert_fusion.8
  120.8 8.5 all-to-all-start.1
  130.1 27.9 %all-to-all-done.1 = bf16[64,1,1,256,32]{3,4,2,1,0:T(8,128)(2,1)} async-done(((bf16[64,1,1,256,32]{3,4,2,1,0:T(8,128)(2,1)}), bf16[64,1,1,256,32]{3,4,2,1,0:T(8,128)(2,1)}, u32[]{:S(2)}, u32[]{:S(2)}) %all-to-all-start.1) | async-done | bytes 1048608 | tf_op jit(solution)/shard_map/all_to_all | solution.py:21
  159.7 1.9 convolution_bitcast_fusion.8
  161.5 1.8 copy.89
  163.5 61.8 %all-reduce.16.cloned.1.call-done = f32[1,256,256]{1,0,2:T(1,128)} async-done(((f32[1,256,256]{1,0,2:T(1,128)}), f32[1,256,256]{1,0,2:T(1,128)}) %all-reduce.16.cloned.1.call-update) | async-done | bytes 262160
  226.0 1.7 bitcast_convert_fusion.7
  227.8 36.9 %all_to_all.50 = bf16[64,1,1,256,32]{3,4,2,1,0:T(8,128)(2,1)S(1)} all-to-all(bf16[64,1,1,256,32]{3,4,2,1,0:T(8,128)(2,1)S(1)} %stack.115), channel_id=1, replica_groups=mesh['leaf'=4,'row'=8,'col'=8] {'row','col'}, dimensions={0} | all-to-all | bytes 2097152 | tf_op jit(solution)/shard_map/all_to_all | solution.py:21
  265.5 1.9 convolution_bitcast_fusion.7
  267.4 1.8 copy.92
  269.3 61.8 %all-reduce.18.cloned.1.call-done = f32[1,256,256]{1,0,2:T(1,128)} async-done(((f32[1,256,256]{1,0,2:T(1,128)}), f32[1,256,256]{1,0,2:T(1,128)}) %all-reduce.18.cloned.1.call-update) | async-done | bytes 262160
  331.9 1.7 bitcast_convert_fusion.6
  334.7 8.5 all-to-all-start.3
  343.8 28.1 %all-to-all-done.3 = bf16[64,1,1,256,32]{3,4,2,1,0:T(8,128)(2,1)} async-done(((bf16[64,1,1,256,32]{3,4,2,1,0:T(8,128)(2,1)}), bf16[64,1,1,256,32]{3,4,2,1,0:T(8,128)(2,1)}, u32[]{:S(2)}, u32[]{:S(2)}) %all-to-all-start.3) | async-done | bytes 1048608 | tf_op jit(solution)/shard_map/all_to_all | solution.py:21
  373.5 2.5 convolution_bitcast_fusion
  376.2 43.7 %all-reduce.12.cloned.1.call-done = f32[2,1,256,256]{3,2,0,1:T(8,128)} async-done(((f32[2,1,256,256]{3,2,0,1:T(8,128)}), f32[2,1,256,256]{3,2,0,1:T(8,128)}) %all-reduce.12.cloned.1.call-update) | async-done | bytes 524304 | tf_op jit(solution)/shard_map/psum | solution.py:88
  421.7 1.1 constant_dynamic-slice_fusion.10
  422.9 66.2 %all-reduce.20.cloned.1.call-done = f32[1,256,256]{1,0,2:T(1,128)} async-done(((f32[1,256,256]{1,0,2:T(1,128)}), f32[1,256,256]{1,0,2:T(1,128)}) %all-reduce.20.cloned.1.call-update) | async-done | bytes 262160
  489.9 1.7 bitcast_convert_fusion.5
  492.7 8.5 all-to-all-start.4
  501.2 1.9 broadcast_multiply_fusion
  503.2 26.7 %all-to-all-done.4 = bf16[64,1,1,256,32]{3,4,2,1,0:T(8,128)(2,1)} async-done(((bf16[64,1,1,256,32]{3,4,2,1,0:T(8,128)(2,1)}), bf16[64,1,1,256,32]{3,4,2,1,0:T(8,128)(2,1)}, u32[]{:S(2)}, u32[]{:S(2)}) %all-to-all-start.4) | async-done | bytes 1048608 | tf_op jit(solution)/shard_map/all_to_all | solution.py:21
  529.9 1.3 fusion.1
  532.1 61.8 %all-reduce.22.cloned.1.call-done = f32[1,256,256]{1,0,2:T(1,128)} async-done(((f32[1,256,256]{1,0,2:T(1,128)}), f32[1,256,256]{1,0,2:T(1,128)}) %all-reduce.22.cloned.1.call-update) | async-done | bytes 262160
  594.7 1.9 bitcast_convert_fusion.4
  596.7 36.9 %all_to_all.51 = bf16[64,1,1,256,32]{3,4,2,1,0:T(8,128)(2,1)S(1)} all-to-all(bf16[64,1,1,256,32]{3,4,2,1,0:T(8,128)(2,1)S(1)} %stack.122), channel_id=1, replica_groups=mesh['leaf'=4,'row'=8,'col'=8] {'row','col'}, dimensions={0} | all-to-all | bytes 2097152 | tf_op jit(solution)/shard_map/all_to_all | solution.py:21
  633.6 1.8 convolution_bitcast_fusion.9
  635.5 29.9 %reduce-scatter.6.cloned.1.call-done = f32[1,256,32]{1,2,0:T(8,128)} async-done(((f32[1,256,256]{1,2,0:T(8,128)}), f32[1,256,32]{1,2,0:T(8,128)}) %reduce-scatter.6.cloned.1.call-update) | async-done | bytes 32784 | tf_op jit(solution)/shard_map/reduce_scatter | solution.py:17
  665.4 1.7 bitcast_convert_fusion.3
  667.1 1.1 stack.123
  668.2 8.4 all-to-all-start.6
  676.8 2.4 bitcast_multiply_fusion.3
  679.2 26.1 %all-to-all-done.6 = bf16[64,1,1,256,32]{3,4,2,1,0:T(8,128)(2,1)} async-done(((bf16[64,1,1,256,32]{3,4,2,1,0:T(8,128)(2,1)}), bf16[64,1,1,256,32]{3,4,2,1,0:T(8,128)(2,1)}, u32[]{:S(2)}, u32[]{:S(2)}) %all-to-all-start.6) | async-done | bytes 1048608 | tf_op jit(solution)/shard_map/all_to_all | solution.py:21
  706.3 1.9 convolution_bitcast_fusion.3
  708.3 29.9 %reduce-scatter.8.cloned.1.call-done = f32[1,256,32]{1,2,0:T(8,128)} async-done(((f32[1,256,256]{1,2,0:T(8,128)}), f32[1,256,32]{1,2,0:T(8,128)}) %reduce-scatter.8.cloned.1.call-update) | async-done | bytes 32784 | tf_op jit(solution)/shard_map/reduce_scatter | solution.py:17
  738.2 1.7 bitcast_convert_fusion.2
  739.9 1.1 stack.127
  741.1 8.5 all-to-all-start.7
  749.7 1.9 convolution_bitcast_fusion.4
  751.6 26.7 %all-to-all-done.7 = bf16[64,1,1,256,32]{3,4,2,1,0:T(8,128)(2,1)} async-done(((bf16[64,1,1,256,32]{3,4,2,1,0:T(8,128)(2,1)}), bf16[64,1,1,256,32]{3,4,2,1,0:T(8,128)(2,1)}, u32[]{:S(2)}, u32[]{:S(2)}) %all-to-all-start.7) | async-done | bytes 1048608 | tf_op jit(solution)/shard_map/all_to_all | solution.py:21
  779.2 1.9 fusion
  781.1 29.9 %reduce-scatter.10.cloned.1.call-done = f32[1,256,32]{1,2,0:T(8,128)} async-done(((f32[1,256,256]{1,2,0:T(8,128)}), f32[1,256,32]{1,2,0:T(8,128)}) %reduce-scatter.10.cloned.1.call-update) | async-done | bytes 32784 | tf_op jit(solution)/shard_map/reduce_scatter | solution.py:17
  811.0 1.7 bitcast_convert_fusion.1
  812.7 1.1 stack.128
  813.9 8.4 all-to-all-start.8
  823.0 27.9 %all-to-all-done.8 = bf16[64,1,1,256,32]{3,4,2,1,0:T(8,128)(2,1)} async-done(((bf16[64,1,1,256,32]{3,4,2,1,0:T(8,128)(2,1)}), bf16[64,1,1,256,32]{3,4,2,1,0:T(8,128)(2,1)}, u32[]{:S(2)}, u32[]{:S(2)}) %all-to-all-start.8) | async-done | bytes 1048608 | tf_op jit(solution)/shard_map/all_to_all | solution.py:21
  852.6 1.2 convolution_bitcast_fusion.2
  853.8 1.9 fusion.5
  855.8 29.9 %reduce-scatter.12.cloned.1.call-done = f32[1,256,32]{1,2,0:T(8,128)} async-done(((f32[1,256,256]{1,2,0:T(8,128)}), f32[1,256,32]{1,2,0:T(8,128)}) %reduce-scatter.12.cloned.1.call-update) | async-done | bytes 32784 | tf_op jit(solution)/shard_map/reduce_scatter | solution.py:17
  885.8 1.7 bitcast_convert_fusion
  887.6 36.7 %all_to_all.52 = bf16[64,1,1,256,32]{3,4,2,1,0:T(8,128)(2,1)S(1)} all-to-all(bf16[64,1,1,256,32]{3,4,2,1,0:T(8,128)(2,1)S(1)} %stack.132), channel_id=1, replica_groups=mesh['leaf'=4,'row'=8,'col'=8] {'row','col'}, dimensions={0} | all-to-all | bytes 2097152 | tf_op jit(solution)/shard_map/all_to_all | solution.py:21
  925.0 1.4 convolution_bitcast_fusion.1
  926.4 1.9 fusion.3
  929.0 29.3 %reduce-scatter.14.cloned.1.call-done = f32[1,256,32]{1,2,0:T(8,128)} async-done(((f32[1,256,256]{1,2,0:T(8,128)}), f32[1,256,32]{1,2,0:T(8,128)}) %reduce-scatter.14.cloned.1.call-update) | async-done | bytes 32784 | tf_op jit(solution)/shard_map/reduce_scatter | solution.py:17
  959.4 1.5 maximum_bitcast_fusion.11
  (103 shorter events, 27.6 us)
Async XLA Ops:
  7.2 1.2 copy-start
  8.4 16.1 %copy-start.10 = (s32[1,4,1,4,1]{3,4,2,1,0:T(1,128)S(1)}, s32[1,4,1,4,1]{3,4,2,1,0:T(1,128)}, u32[]{:S(2)}) copy-start(s32[1,4,1,4,1]{3,4,2,1,0:T(1,128)} %param.22) | copy-start | bytes 196
  8.6 16.0 %copy-start.1 = (f32[1,4,1,256,32]{4,3,2,1,0:T(8,128)}, f32[1,4,1,256,32]{4,3,2,1,0:T(8,128)S(1)}, u32[]{:S(2)}) copy-start(f32[1,4,1,256,32]{4,3,2,1,0:T(8,128)S(1)} %constant_dynamic-slice_fusion.11) | copy-start | bytes 393220
  12.3 40.9 %all-to-all-start = ((bf16[64,1,1,256,32]{3,4,2,1,0:T(8,128)(2,1)}), bf16[64,1,1,256,32]{3,4,2,1,0:T(8,128)(2,1)}, u32[]{:S(2)}, u32[]{:S(2)}) async-start(bf16[64,1,1,256,32]{3,4,2,1,0:T(8,128)(2,1)} %stack.110), calls=%async_computation | async-start | bytes 2097152 | tf_op jit(solution)/shard_map/all_to_all | solution.py:21
  24.5 92.7 %all-reduce.14.cloned.1.call-start = ((), (), s32[]{:S(2)}) async-start(), calls=%async_computation.21 | async-start | bytes 524288
  120.8 37.2 %all-to-all-start.1 = ((bf16[64,1,1,256,32]{3,4,2,1,0:T(8,128)(2,1)}), bf16[64,1,1,256,32]{3,4,2,1,0:T(8,128)(2,1)}, u32[]{:S(2)}, u32[]{:S(2)}) async-start(bf16[64,1,1,256,32]{3,4,2,1,0:T(8,128)(2,1)} %stack.112), calls=%async_computation.1 | async-start | bytes 2097152 | tf_op jit(solution)/shard_map/all_to_all | solution.py:21
  129.3 96.0 %all-reduce.16.cloned.1.call-start = ((), (), s32[]{:S(2)}) async-start(), calls=%async_computation.22 | async-start | bytes 524288
  163.4 167.8 %all-reduce.18.cloned.1.call-start = ((), (), s32[]{:S(2)}) async-start(), calls=%async_computation.23 | async-start | bytes 524288
  163.5 102.0 %copy-start.4 = (bf16[1,256,256]{2,1,0:T(8,128)(2,1)S(1)}, bf16[1,256,256]{2,1,0:T(8,128)(2,1)}, u32[]{:S(2)}) copy-start(bf16[1,256,256]{2,1,0:T(8,128)(2,1)} %copy.85) | copy-start | bytes 393220
  267.4 75.8 %copy-start.11 = (s32[1,2,1,4,1]{3,4,2,1,0:T(1,128)S(1)}, s32[1,2,1,4,1]{3,4,2,1,0:T(1,128)}, u32[]{:S(2)}) copy-start(s32[1,2,1,4,1]{3,4,2,1,0:T(1,128)} %param.23) | copy-start | bytes 100
  269.3 104.2 %copy-start.5 = (bf16[1,256,256]{2,1,0:T(8,128)(2,1)S(1)}, bf16[1,256,256]{2,1,0:T(8,128)(2,1)}, u32[]{:S(2)}) copy-start(bf16[1,256,256]{2,1,0:T(8,128)(2,1)} %copy.88) | copy-start | bytes 393220
  334.7 37.2 %all-to-all-start.3 = ((bf16[64,1,1,256,32]{3,4,2,1,0:T(8,128)(2,1)}), bf16[64,1,1,256,32]{3,4,2,1,0:T(8,128)(2,1)}, u32[]{:S(2)}, u32[]{:S(2)}) async-start(bf16[64,1,1,256,32]{3,4,2,1,0:T(8,128)(2,1)} %stack.118), calls=%async_computation.3 | async-start | bytes 2097152 | tf_op jit(solution)/shard_map/all_to_all | solution.py:21
  343.2 76.7 %all-reduce.12.cloned.1.call-start = ((), (), s32[]{:S(2)}) async-start(), calls=%async_computation.15 | async-start | bytes 1048576 | tf_op jit(solution)/shard_map/psum | solution.py:88
  376.1 113.0 %all-reduce.20.cloned.1.call-start = ((), (), s32[]{:S(2)}) async-start(), calls=%async_computation.24 | async-start | bytes 524288
  421.7 79.5 %copy-start.12 = (s32[2,1,2,1]{2,3,1,0:T(1,128)S(1)}, s32[2,1,2,1]{2,3,1,0:T(1,128)}, u32[]{:S(2)}) copy-start(s32[2,1,2,1]{2,3,1,0:T(1,128)} %param.25) | copy-start | bytes 52
  492.7 37.2 %all-to-all-start.4 = ((bf16[64,1,1,256,32]{3,4,2,1,0:T(8,128)(2,1)}), bf16[64,1,1,256,32]{3,4,2,1,0:T(8,128)(2,1)}, u32[]{:S(2)}, u32[]{:S(2)}) async-start(bf16[64,1,1,256,32]{3,4,2,1,0:T(8,128)(2,1)} %stack.121), calls=%async_computation.4 | async-start | bytes 2097152 | tf_op jit(solution)/shard_map/all_to_all | solution.py:21
  501.1 92.8 %all-reduce.22.cloned.1.call-start = ((), (), s32[]{:S(2)}) async-start(), calls=%async_computation.25 | async-start | bytes 524288
  532.0 133.4 %reduce-scatter.6.cloned.1.call-start = ((), (), s32[]{:S(2)}) async-start(), calls=%async_computation.16 | async-start | bytes 294912 | tf_op jit(solution)/shard_map/reduce_scatter | solution.py:17
  596.6 68.8 %copy-start.3 = (f32[32,256]{1,0:T(8,128)S(1)}, f32[32,256]{1,0:T(8,128)}, u32[]{:S(2)}) copy-start(f32[32,256]{1,0:T(8,128)} %get-tuple-element.28) | copy-start | bytes 98308
  633.6 43.1 %copy-start.13 = (s32[1,4,1,2,1]{1,4,3,2,0:T(1,128)S(1)}, s32[1,4,1,2,1]{1,4,3,2,0:T(1,128)}, u32[]{:S(2)}) copy-start(s32[1,4,1,2,1]{1,4,3,2,0:T(1,128)} %param.24) | copy-start | bytes 100
  668.2 37.1 %all-to-all-start.6 = ((bf16[64,1,1,256,32]{3,4,2,1,0:T(8,128)(2,1)}), bf16[64,1,1,256,32]{3,4,2,1,0:T(8,128)(2,1)}, u32[]{:S(2)}, u32[]{:S(2)}) async-start(bf16[64,1,1,256,32]{3,4,2,1,0:T(8,128)(2,1)} %stack.123), calls=%async_computation.7 | async-start | bytes 2097152 | tf_op jit(solution)/shard_map/all_to_all | solution.py:21
  676.6 61.6 %reduce-scatter.8.cloned.1.call-start = ((), (), s32[]{:S(2)}) async-start(), calls=%async_computation.17 | async-start | bytes 294912 | tf_op jit(solution)/shard_map/reduce_scatter | solution.py:17
  741.1 37.3 %all-to-all-start.7 = ((bf16[64,1,1,256,32]{3,4,2,1,0:T(8,128)(2,1)}), bf16[64,1,1,256,32]{3,4,2,1,0:T(8,128)(2,1)}, u32[]{:S(2)}, u32[]{:S(2)}) async-start(bf16[64,1,1,256,32]{3,4,2,1,0:T(8,128)(2,1)} %stack.127), calls=%async_computation.9 | async-start | bytes 2097152 | tf_op jit(solution)/shard_map/all_to_all | solution.py:21
  749.6 61.4 %reduce-scatter.10.cloned.1.call-start = ((), (), s32[]{:S(2)}) async-start(), calls=%async_computation.18 | async-start | bytes 294912 | tf_op jit(solution)/shard_map/reduce_scatter | solution.py:17
  813.9 37.1 %all-to-all-start.8 = ((bf16[64,1,1,256,32]{3,4,2,1,0:T(8,128)(2,1)}), bf16[64,1,1,256,32]{3,4,2,1,0:T(8,128)(2,1)}, u32[]{:S(2)}, u32[]{:S(2)}) async-start(bf16[64,1,1,256,32]{3,4,2,1,0:T(8,128)(2,1)} %stack.128), calls=%async_computation.11 | async-start | bytes 2097152 | tf_op jit(solution)/shard_map/all_to_all | solution.py:21
  822.2 63.5 %reduce-scatter.12.cloned.1.call-start = ((), (), s32[]{:S(2)}) async-start(), calls=%async_computation.19 | async-start | bytes 294912 | tf_op jit(solution)/shard_map/reduce_scatter | solution.py:17
  852.6 33.2 %copy-start.2 = (f32[32,256]{1,0:T(8,128)S(1)}, f32[32,256]{1,0:T(8,128)}, u32[]{:S(2)}) copy-start(f32[32,256]{1,0:T(8,128)} %get-tuple-element.22) | copy-start | bytes 98308
  855.8 102.5 %reduce-scatter.14.cloned.1.call-start = ((), (), s32[]{:S(2)}) async-start(), calls=%async_computation.20 | async-start | bytes 294912 | tf_op jit(solution)/shard_map/reduce_scatter | solution.py:17
  925.0 3.3 copy-start.7
  925.0 3.4 copy-start.8
  925.0 33.3 %copy-start.6 = (f32[32,256]{1,0:T(8,128)S(1)}, f32[32,256]{1,0:T(8,128)}, u32[]{:S(2)}) copy-start(f32[32,256]{1,0:T(8,128)} %get-tuple-element.20) | copy-start | bytes 98308
  925.0 34.4 %copy-start.9 = (f32[32,256]{1,0:T(8,128)S(1)}, f32[32,256]{1,0:T(8,128)}, u32[]{:S(2)}) copy-start(f32[32,256]{1,0:T(8,128)} %get-tuple-element.34) | copy-start | bytes 98308
Sparse Core Ops, SparseCore 0:
  55.3 61.8 all-reduce.13
  163.5 61.7 all-reduce.15
  269.4 61.7 all-reduce.17
  376.2 43.6 all-reduce.11
  422.1 66.9 all-reduce.19
  532.1 61.7 all-reduce.21
  635.6 29.7 reduce-scatter.5
  708.4 29.7 reduce-scatter.7
  781.3 29.6 reduce-scatter.9
  855.9 29.7 reduce-scatter.11
  928.5 29.7 reduce-scatter.13
